TPU v7x, 512 devices: a whole 4x8x8 slice. The times are simulated.
512 devices in a mesh: atom: 64 (over y, x, z_hi), ka: 8 (over z_lo, core).
Axes of the slice: x: 4, y: 8, z: 8 (z_hi: 2, z_lo: 4; z = z_hi * 4 + z_lo), core: 2. Of those that a mesh axis runs over, the one named last changes fastest.
Arguments:
- features: bfloat16 [131072, 256], P('atom'), may hold values from -6 to 6
- positions: float32 [3, 131072], P(None, 'atom'), may hold values from 0 to 1
- k_indices: int32 [3, 4096], P(None, 'ka'), may hold values from -8 to 8
- species: int32 [131072], P('atom'), may hold values from 0 to 7
- brick_counts: int32 [64], P('atom'), may hold values from 1024 to 2048, as said below
- smearing: float32 [256], replicated, may hold values from 0.01 to 0.03
- teacher_charge: float32 [256], replicated, may hold values from -0.375 to 0.375
- norm_gain: float32 [256], replicated, may hold values from 0.5 to 1.5
- w_mix: bfloat16 [256, 256], replicated, may hold values from -0.375 to 0.375
- w_read: float32 [256], replicated, may hold values from -0.375 to 0.375
- w_student: bfloat16 [256, 128], replicated, may hold values from -0.375 to 0.375
- species_embed: float32 [8, 128], replicated, may hold values from -3 to 3
- w_charge: float32 [128], replicated, may hold values from -0.5 to 0.5
- species_bias: float32 [8], replicated, may hold values from -3 to 3
- student_smear: float32 [1], replicated, may hold values from 0.05 to 0.15
Outputs:
- teacher_features: bfloat16 [131072, 256], P(('atom', 'ka'))
- teacher_forces: float32 [3, 131072], P(None, ('atom', 'ka'))
- student_forces: float32 [3, 131072], P(None, ('atom', 'ka'))
- student_energy: float32 [131072], P(('atom', 'ka'))
- distill_loss: float32 [], replicated
Inputs may be any that keep to these rules, and one draw needn't show every extreme that they name: The first brick_counts[b] atom slots of brick b hold real atoms and the rest are padding; some brick is full in every draw.
All inputs are finite; a program needn't handle non-finite values.
Results may differ from a plain program's by a relative error of at most 0.0075.
Values sent between devices are 32-bit elements; how exact they have to be, the bound alone decides.
No kernel may reach another device: no remote copies, remote signals or barrier semaphores. Data moves between devices by JAX's collectives and lax.ppermute only.
A program may use at most 64 MiB of HBM per device.

v0:
```python
import math
import jax
import jax.numpy as jnp
from jax import lax
from jax.sharding import PartitionSpec as P

TWO_PI = 2.0 * math.pi
SCREEN = 20.0
HIGHEST_PRECISION = lax.Precision.HIGHEST


def phase_table(positions, k_indices):
    k_float = k_indices.astype(jnp.float32)
    products = (
        positions[0][:, None] * k_float[0][None, :]
        + positions[1][:, None] * k_float[1][None, :]
        + positions[2][:, None] * k_float[2][None, :]
    )
    angles = TWO_PI * products
    return jnp.concatenate([jnp.cos(angles), jnp.sin(angles)], axis=1).astype(jnp.bfloat16)


def k_geometry(k_indices):
    k_vectors = TWO_PI * k_indices.astype(jnp.float32)
    k_square = (
        k_vectors[0] * k_vectors[0] + k_vectors[1] * k_vectors[1] + k_vectors[2] * k_vectors[2]
    )
    return (k_vectors, k_square)


def teacher_kernel(k_square, smearing, inv_root):
    spread = (smearing * smearing)[None, :]
    return jnp.exp(-0.5 * k_square[:, None] * spread) / (k_square[:, None] + SCREEN) * inv_root


def student_table(k_vectors, k_square, sums, student_smear, inv_root, k_width):
    spread = student_smear[0] * student_smear[0]
    kernel = jnp.exp(-0.5 * k_square * spread) / (k_square + SCREEN) * inv_root
    cos_part = kernel * sums[:k_width]
    sin_part = kernel * sums[k_width:]
    upper_rows = jnp.stack(
        [
            cos_part,
            -(k_vectors[0] * sin_part),
            -(k_vectors[1] * sin_part),
            -(k_vectors[2] * sin_part),
        ],
        axis=1,
    )
    lower_rows = jnp.stack(
        [sin_part, k_vectors[0] * cos_part, k_vectors[1] * cos_part, k_vectors[2] * cos_part],
        axis=1,
    )
    return jnp.concatenate([upper_rows, lower_rows], axis=0).astype(jnp.bfloat16)


def student_charge(features, species, live_mask, w_student, species_embed, w_charge, species_bias):
    onehot = (
        species[:, None] == jnp.arange(species_embed.shape[0], dtype=jnp.int32)[None, :]
    ).astype(jnp.float32)
    inner_sum = jnp.dot(features, w_student, preferred_element_type=jnp.float32) + jnp.dot(
        onehot, species_embed, precision=HIGHEST_PRECISION
    )
    hidden = jax.nn.silu(inner_sum)
    return (
        jnp.dot(hidden, w_charge, precision=HIGHEST_PRECISION)
        + jnp.dot(onehot, species_bias, precision=HIGHEST_PRECISION)
    ) * live_mask


def finish(
    potential, teacher_force, student_part, features, charge, live_mask, norm_gain, w_mix, w_read
):
    mean_square = jnp.mean(potential * potential, axis=1, keepdims=True)
    normed = (potential * lax.rsqrt(mean_square + 1e-06) * norm_gain[None, :]).astype(jnp.bfloat16)
    update = jax.nn.silu(jnp.dot(normed, w_mix, preferred_element_type=jnp.float32))
    combined = features.astype(jnp.float32) + update
    teacher_energy = jnp.dot(combined, w_read, precision=HIGHEST_PRECISION)
    student_energy = 0.5 * charge * student_part[:, 0]
    forces = charge[:, None] * student_part[:, 1:4]
    misfit = (student_energy - teacher_energy) ** 2 + jnp.sum(
        (forces - teacher_force) ** 2, axis=1
    ) / 3.0
    return (
        combined.astype(jnp.bfloat16),
        teacher_force,
        forces,
        student_energy,
        live_mask * misfit,
    )


def local(
    features,
    positions,
    k_indices,
    species,
    brick_counts,
    smearing,
    teacher_charge,
    norm_gain,
    w_mix,
    w_read,
    w_student,
    species_embed,
    w_charge,
    species_bias,
    student_smear,
):
    atom_rows = features.shape[0]
    k_width = k_indices.shape[1]
    inv_root = 1.0 / math.sqrt(atom_rows * lax.axis_size("atom"))
    live_mask = (jnp.arange(atom_rows, dtype=jnp.int32) < brick_counts[0]).astype(jnp.float32)
    masked = features * live_mask.astype(jnp.bfloat16)[:, None]
    charge = student_charge(
        features, species, live_mask, w_student, species_embed, w_charge, species_bias
    )
    charge_low = charge.astype(jnp.bfloat16)
    phases = phase_table(positions, k_indices)
    factor = lax.dot_general(
        phases, masked, (((0,), (0,)), ((), ())), preferred_element_type=jnp.float32
    )
    charge_sum = jnp.dot(charge_low, phases, preferred_element_type=jnp.float32)
    factor, charge_sum = lax.psum((factor, charge_sum), "atom")
    k_vectors, k_square = k_geometry(k_indices)
    kernel = teacher_kernel(k_square, smearing, inv_root)
    weighted = (jnp.concatenate([kernel, kernel], axis=0) * factor).astype(jnp.bfloat16)
    potential = jnp.dot(phases, weighted, preferred_element_type=jnp.float32)
    charged = (features.astype(jnp.float32) * teacher_charge[None, :]).astype(jnp.bfloat16)
    contracted = lax.dot_general(
        charged, weighted, (((1,), (1,)), ((), ())), preferred_element_type=jnp.float32
    )
    cosines = phases[:, :k_width].astype(jnp.float32)
    sines = phases[:, k_width:].astype(jnp.float32)
    force_terms = sines * contracted[:, :k_width] - cosines * contracted[:, k_width:]
    teacher_force = jnp.dot(force_terms, k_vectors.T, precision=HIGHEST_PRECISION)
    table = student_table(k_vectors, k_square, charge_sum, student_smear, inv_root, k_width)
    student_part = jnp.dot(phases, table, preferred_element_type=jnp.float32)
    share_rows = atom_rows // lax.axis_size("ka")
    row_start = lax.axis_index("ka") * share_rows

    def own_rows(values):
        return lax.dynamic_slice_in_dim(values, row_start, share_rows, 0)

    potential, teacher_force, student_part = lax.psum(
        (potential, teacher_force, student_part), "ka"
    )
    whole_rows = finish(
        potential,
        teacher_force,
        student_part,
        features,
        charge,
        live_mask,
        norm_gain,
        w_mix,
        w_read,
    )
    outputs = (
        own_rows(whole_rows[0]),
        own_rows(whole_rows[1]),
        own_rows(whole_rows[2]),
        own_rows(whole_rows[3]),
        own_rows(whole_rows[4]),
    )
    teacher_features, teacher_out, forces, student_energy, misfit = outputs
    loss_sum, live_sum = lax.psum((jnp.sum(misfit), jnp.sum(own_rows(live_mask))), ("atom", "ka"))
    return (teacher_features, teacher_out.T, forces.T, student_energy, loss_sum / live_sum)


def solution(mesh):
    in_specs = (
        P("atom", None),
        P(None, "atom"),
        P(None, "ka"),
        P("atom"),
        P("atom"),
        P(),
        P(),
        P(),
        P(),
        P(),
        P(),
        P(),
        P(),
        P(),
        P(),
    )
    out_specs = (
        P(("atom", "ka"), None),
        P(None, ("atom", "ka")),
        P(None, ("atom", "ka")),
        P(("atom", "ka")),
        P(),
    )
    return jax.shard_map(local, mesh=mesh, in_specs=in_specs, out_specs=out_specs, check_vma=False)
```

profile of v0, /device:TPU:1, one launch (start us, length us, event | category | flops | bytes accessed | tf_op | source)
XLA Modules:
  0.0 1086.3 jit_solution(1658053746841825445)
XLA Ops:
  7.2 0.0 copy-start
  7.2 0.0 all-reduce.5.cloned.1.call-start
  8.0 0.7 convert_element_type.47
  8.7 0.9 fusion.58
  9.6 17.6 %cosine_convert_fusion = (bf16[2048,512]{1,0:T(8,128)(2,1)S(1)}, bf16[2048,512]{1,0:T(8,128)(2,1)S(1)}) fusion(f32[512]{0:T(512)S(1)} %bitcast.54, f32[2048]{0:T(1024)S(1)} %bitcast.39, f32[512]{0:T(512)S(1)} %bitcast.56, f32[2048]{0:T(1024)S(1)} %bitcast.41, f32[512]{0:T(512)S(1)} %bitcast.52, f32[2048]{0:T(1024)S(1)} %bitcast.37), kind=kLoop, calls=%fused_computation.8 | loop fusion | flops 8388608 | bytes 4225024 | tf_op jit(solution)/shard_map/slice | solution.py:133
  27.3 1.3 copy-done.3
  28.6 2.6 fusion.20
  31.2 0.0 all-reduce.5.cloned.1.call-update
  31.3 0.0 all-reduce.7.cloned.1.call-start
  32.0 0.4 fusion.61
  32.4 0.7 fusion.16
  33.2 1.0 convolution_add_fusion
  34.2 1.2 fusion.10
  35.4 0.6 fusion.55
  36.0 203.7 %psum.52 = f32[1024]{0:T(1024)S(1)} all-reduce(f32[1024]{0:T(1024)S(1)} %bitcast.60), channel_id=1, replica_groups=mesh['atom'=64,'ka'=8] {'atom'}, use_global_device_ids=true, to_apply=%region_4.5 | all-reduce | flops 1024 | bytes 8192 | tf_op jit(solution)/shard_map/psum | solution.py:124
  239.8 0.2 divide_multiply_fusion
  240.0 599.3 %all-reduce.5.cloned.1.call-done = f32[1024,256]{1,0:T(8,128)} async-done(((f32[1024,256]{1,0:T(8,128)}), f32[1024,256]{1,0:T(8,128)}) %all-reduce.5.cloned.1.call-update) | async-done | bytes 1048592 | tf_op jit(solution)/shard_map/psum | solution.py:124
  839.4 5.1 fusion.53
  844.5 0.0 all-reduce.7.cloned.1.call-update
  844.6 0.7 dynamic-slice_reduce_fusion
  845.3 3.5 fusion.26
  848.8 1.3 fusion.7
  850.1 20.6 %fusion.1 = f32[2048,3]{0,1:T(4,128)S(1)} fusion(f32[2048,1024]{1,0:T(8,128)S(1)} %fusion.7, s32[3,512]{1,0:T(4,128)S(1)} %copy-done.7, f32[512]{0:T(512)S(1)} %bitcast.55, f32[2048]{0:T(1024)S(1)} %bitcast.40, f32[512]{0:T(512)S(1)} %bitcast.57, f32[2048]{0:T(1024)S(1)} %bitcast.42, f32[512]{0:T(512)S(1)} %bitcast.53, f32[2048]{0:T(1024)S(1)} %bitcast.38), kind=kOutput, calls=%fused_computation.2 | convolution fusion | flops 51383296 | bytes 8450048 | tf_op jit(solution)/shard_map/dot_general | solution.py:136
  870.8 68.6 %all-reduce.1 = (f32[2048,3]{0,1:T(4,128)S(1)}, f32[2048,4]{0,1:T(4,128)S(1)}) all-reduce(f32[2048,3]{0,1:T(4,128)S(1)} %fusion.1, f32[2048,4]{0,1:T(4,128)S(1)} %fusion.26), channel_id=1, replica_groups=mesh['atom'=64,'ka'=8] {'ka'}, use_global_device_ids=true, to_apply=%region_3.4 | all-reduce | flops 14336 | bytes 114688 | tf_op jit(solution)/shard_map/psum | solution.py:145
  939.4 0.6 dynamic-slice_bitcast_fusion
  940.0 28.5 %all-reduce.7.cloned.1.call-done = f32[2048,256]{1,0:T(8,128)} async-done(((f32[2048,256]{1,0:T(8,128)}), f32[2048,256]{1,0:T(8,128)}) %all-reduce.7.cloned.1.call-update) | async-done | bytes 2097168 | tf_op jit(solution)/shard_map/psum | solution.py:145
  968.6 1.9 multiply_reduce_fusion
  970.5 2.4 convert_add_fusion
  973.0 0.7 dynamic-slice_convert_fusion
  973.7 1.9 fusion.62
  975.5 1.3 fusion.45
  976.8 100.2 %all-reduce = (f32[]{:T(128)}, f32[]{:T(128)}) all-reduce(f32[]{:T(128)} %get-tuple-element.9, f32[]{:T(128)} %dynamic-slice_reduce_fusion), channel_id=1, replica_groups=mesh['atom'=64,'ka'=8] {'atom','ka'}, use_global_device_ids=true, to_apply=%region_8.9 | all-reduce | flops 2 | bytes 16 | tf_op jit(solution)/shard_map/psum | solution.py:167
  (53 shorter events, 0.3 us)
Async XLA Ops:
  7.2 963.4 %copy-start = (bf16[256,256]{1,0:T(8,128)(2,1)S(1)}, bf16[256,256]{1,0:T(8,128)(2,1)}, u32[]{:S(2)}) copy-start(bf16[256,256]{1,0:T(8,128)(2,1)} %param.23) | copy-start | bytes 393220
  7.2 21.4 %copy-start.1 = (bf16[2048,256]{1,0:T(8,128)(2,1)S(1)}, bf16[2048,256]{1,0:T(8,128)(2,1)}, u32[]{:S(2)}) copy-start(bf16[2048,256]{1,0:T(8,128)(2,1)} %param.15) | copy-start | bytes 3145732
  7.2 832.2 %all-reduce.5.cloned.1.call-start = ((), (), s32[]{:S(2)}) async-start(), calls=%async_computation | async-start | bytes 2097152 | tf_op jit(solution)/shard_map/psum | solution.py:124
  27.2 1.3 copy-start.3
  27.2 8.1 copy-start.2
  28.6 3.4 copy-start.10
  28.6 3.4 copy-start.6
  28.6 3.8 copy-start.8
  28.6 3.9 copy-start.14
  28.6 4.6 copy-start.9
  31.2 2.9 copy-start.15
  31.3 937.3 %all-reduce.7.cloned.1.call-start = ((), (), s32[]{:S(2)}) async-start(), calls=%async_computation.1 | async-start | bytes 4194304 | tf_op jit(solution)/shard_map/psum | solution.py:145
  32.0 3.4 copy-start.4
  34.1 205.6 %copy-start.7 = (s32[3,512]{1,0:T(4,128)S(1)}, s32[3,512]{1,0:T(4,128)}, u32[]{:S(2)}) copy-start(s32[3,512]{1,0:T(4,128)} %param.17) | copy-start | bytes 18436
  845.3 3.5 copy-start.5
  845.3 3.5 copy-start.11
  850.1 120.4 %copy-start.13 = (f32[256]{0:T(256)S(1)}, f32[256]{0:T(256)}, u32[]{:S(2)}) copy-start(f32[256]{0:T(256)} %param.22) | copy-start | bytes 3076
  970.5 3.1 copy-start.12
Sparse Core Ops, SparseCore 0:
  31.4 807.9 all-reduce.4
  844.6 123.9 all-reduce.6
where the time goes:
time: 1090 us
  waiting for transfers between devices  628 us (58%)
  blocking collectives  372 us (34%)
  matrix products  41.4 us (4%)
  other arithmetic  22.5 us (2%)
  between operations  18.2 us (2%)
    psum x1, waiting for transfers between devices, local(): factor, charge_sum = lax.psum((factor, charge_sum), 'atom')  599 us
    psum x1, blocking collectives, local(): factor, charge_sum = lax.psum((factor, charge_sum), 'atom')  204 us
    psum x1, blocking collectives, local(): lax.psum((jnp.sum(misfit), jnp.sum(own_rows(live_mask))), ('atom', 'ka'))  100 us
    psum x1, blocking collectives, local(): lax.psum((potential, teacher_force, student_part), 'ka')  68.6 us
    psum x1, waiting for transfers between devices, local(): lax.psum((potential, teacher_force, student_part), 'ka')  28.5 us
  transfers between devices with their start and end apart: 2, of which 2 were waited for; matrix products, arithmetic and copies ran while one was open for 3% of the time, Pallas kernels for 0%

commit v1 on v0

--- a/solution.py
+++ b/solution.py
@@ -164,7 +164,9 @@
         own_rows(whole_rows[4]),
     )
     teacher_features, teacher_out, forces, student_energy, misfit = outputs
-    loss_sum, live_sum = lax.psum((jnp.sum(misfit), jnp.sum(own_rows(live_mask))), ("atom", "ka"))
+    loss_sum, live_sum = lax.psum(
+        lax.psum((jnp.sum(misfit), jnp.sum(own_rows(live_mask))), "ka"), "atom"
+    )
     return (teacher_features, teacher_out.T, forces.T, student_energy, loss_sum / live_sum)
 
 

time: 1090 us -> 1220 us (1.12)
  the two profiles are of different devices: /device:TPU:1 before, /device:TPU:32 now
where the time goes in v1:
time: 1220 us
  waiting for transfers between devices  647 us (53%)
  blocking collectives  491 us (40%)
  matrix products  41.4 us (3%)
  other arithmetic  22.6 us (2%)
  between operations  18.2 us (1%)
    psum x1, waiting for transfers between devices, local(): factor, charge_sum = lax.psum((factor, charge_sum), 'atom')  619 us
    psum x1, blocking collectives, local(): factor, charge_sum = lax.psum((factor, charge_sum), 'atom')  226 us
    psum x1, blocking collectives, local(): lax.psum(lax.psum((jnp.sum(misfit), jnp.sum(own_rows(live_mask))), 'ka'),...  221 us
    psum x1, waiting for transfers between devices, local(): lax.psum((potential, teacher_force, student_part), 'ka')  28.4 us
    psum x1, blocking collectives, local(): lax.psum((potential, teacher_force, student_part), 'ka')  26.8 us
  transfers between devices with their start and end apart: 2, of which 2 were waited for; matrix products, arithmetic and copies ran while one was open for 3% of the time, Pallas kernels for 0%

profile of v1, /device:TPU:32, one launch (start us, length us, event | category | flops | bytes accessed | tf_op | source)
XLA Modules:
  0.0 1224.0 jit_solution(15743364662750504225)
XLA Ops:
  7.2 0.0 all-reduce.6.cloned.1.call-start
  8.0 0.7 convert_element_type.47
  8.7 0.9 fusion.58
  9.6 17.6 %cosine_convert_fusion = (bf16[2048,512]{1,0:T(8,128)(2,1)S(1)}, bf16[2048,512]{1,0:T(8,128)(2,1)S(1)}) fusion(f32[512]{0:T(512)S(1)} %bitcast.54, f32[2048]{0:T(1024)S(1)} %bitcast.39, f32[512]{0:T(512)S(1)} %bitcast.56, f32[2048]{0:T(1024)S(1)} %bitcast.41, f32[512]{0:T(512)S(1)} %bitcast.52, f32[2048]{0:T(1024)S(1)} %bitcast.37), kind=kLoop, calls=%fused_computation.8 | loop fusion | flops 8388608 | bytes 4225024 | tf_op jit(solution)/shard_map/slice | solution.py:133
  27.3 1.3 copy-done.3
  28.6 2.6 fusion.20
  31.2 0.0 all-reduce.6.cloned.1.call-update
  31.3 0.0 all-reduce.8.cloned.1.call-start
  32.0 0.4 fusion.61
  32.5 0.7 fusion.16
  33.2 1.0 convolution_add_fusion
  34.2 1.2 fusion.10
  35.4 0.6 fusion.55
  36.1 226.3 %psum.66 = f32[1024]{0:T(1024)S(1)} all-reduce(f32[1024]{0:T(1024)S(1)} %bitcast.60), channel_id=1, replica_groups=mesh['atom'=64,'ka'=8] {'atom'}, use_global_device_ids=true, to_apply=%region_4.5 | all-reduce | flops 1024 | bytes 8192 | tf_op jit(solution)/shard_map/psum | solution.py:124
  262.4 0.2 divide_multiply_fusion
  262.6 618.5 %all-reduce.6.cloned.1.call-done = f32[1024,256]{1,0:T(8,128)} async-done(((f32[1024,256]{1,0:T(8,128)}), f32[1024,256]{1,0:T(8,128)}) %all-reduce.6.cloned.1.call-update) | async-done | bytes 1048592 | tf_op jit(solution)/shard_map/psum | solution.py:124
  881.2 5.1 fusion.53
  886.3 0.0 all-reduce.8.cloned.1.call-update
  886.4 0.8 dynamic-slice_reduce_fusion
  887.2 3.5 fusion.26
  890.7 1.3 fusion.7
  892.0 20.6 %fusion.1 = f32[2048,3]{0,1:T(4,128)S(1)} fusion(f32[2048,1024]{1,0:T(8,128)S(1)} %fusion.7, s32[3,512]{1,0:T(4,128)S(1)} %copy-done.7, f32[512]{0:T(512)S(1)} %bitcast.55, f32[2048]{0:T(1024)S(1)} %bitcast.40, f32[512]{0:T(512)S(1)} %bitcast.57, f32[2048]{0:T(1024)S(1)} %bitcast.42, f32[512]{0:T(512)S(1)} %bitcast.53, f32[2048]{0:T(1024)S(1)} %bitcast.38), kind=kOutput, calls=%fused_computation.2 | convolution fusion | flops 51383296 | bytes 8450048 | tf_op jit(solution)/shard_map/dot_general | solution.py:136
  912.6 26.8 %all-reduce.2 = (f32[2048,3]{0,1:T(4,128)S(1)}, f32[2048,4]{0,1:T(4,128)S(1)}) all-reduce(f32[2048,3]{0,1:T(4,128)S(1)} %fusion.1, f32[2048,4]{0,1:T(4,128)S(1)} %fusion.26), channel_id=1, replica_groups=mesh['atom'=64,'ka'=8] {'ka'}, use_global_device_ids=true, to_apply=%region_3.4 | all-reduce | flops 14336 | bytes 114688 | tf_op jit(solution)/shard_map/psum | solution.py:145
  939.5 0.6 dynamic-slice_bitcast_fusion
  940.1 28.4 %all-reduce.8.cloned.1.call-done = f32[2048,256]{1,0:T(8,128)} async-done(((f32[2048,256]{1,0:T(8,128)}), f32[2048,256]{1,0:T(8,128)}) %all-reduce.8.cloned.1.call-update) | async-done | bytes 2097168 | tf_op jit(solution)/shard_map/psum | solution.py:145
  968.5 1.9 multiply_reduce_fusion
  970.5 2.4 convert_add_fusion
  972.9 0.7 dynamic-slice_convert_fusion
  973.6 1.9 fusion.62
  975.5 1.3 fusion.45
  976.7 16.9 %all-reduce.1 = (f32[]{:T(128)}, f32[]{:T(128)}) all-reduce(f32[]{:T(128)} %get-tuple-element.11, f32[]{:T(128)} %dynamic-slice_reduce_fusion), channel_id=1, replica_groups=mesh['atom'=64,'ka'=8] {'ka'}, use_global_device_ids=true, to_apply=%region_8.9 | all-reduce | flops 2 | bytes 16 | tf_op jit(solution)/shard_map/psum | solution.py:168
  993.6 221.2 %all-reduce = (f32[]{:T(128)}, f32[]{:T(128)}) all-reduce(f32[]{:T(128)} %get-tuple-element.7, f32[]{:T(128)} %get-tuple-element.8), channel_id=1, replica_groups=mesh['atom'=64,'ka'=8] {'atom'}, use_global_device_ids=true, to_apply=%region_9.10 | all-reduce | flops 2 | bytes 16 | tf_op jit(solution)/shard_map/psum | solution.py:167
  (54 shorter events, 0.3 us)
Async XLA Ops:
  7.2 963.3 %copy-start = (bf16[256,256]{1,0:T(8,128)(2,1)S(1)}, bf16[256,256]{1,0:T(8,128)(2,1)}, u32[]{:S(2)}) copy-start(bf16[256,256]{1,0:T(8,128)(2,1)} %param.23) | copy-start | bytes 393220
  7.2 21.4 %copy-start.1 = (bf16[2048,256]{1,0:T(8,128)(2,1)S(1)}, bf16[2048,256]{1,0:T(8,128)(2,1)}, u32[]{:S(2)}) copy-start(bf16[2048,256]{1,0:T(8,128)(2,1)} %param.15) | copy-start | bytes 3145732
  7.2 874.0 %all-reduce.6.cloned.1.call-start = ((), (), s32[]{:S(2)}) async-start(), calls=%async_computation | async-start | bytes 2097152 | tf_op jit(solution)/shard_map/psum | solution.py:124
  27.2 1.3 copy-start.3
  27.2 8.2 copy-start.2
  28.6 3.4 copy-start.10
  28.6 3.4 copy-start.6
  28.6 3.9 copy-start.8
  28.6 3.9 copy-start.14
  28.6 4.6 copy-start.9
  31.2 2.9 copy-start.15
  31.3 937.3 %all-reduce.8.cloned.1.call-start = ((), (), s32[]{:S(2)}) async-start(), calls=%async_computation.1 | async-start | bytes 4194304 | tf_op jit(solution)/shard_map/psum | solution.py:145
  32.0 3.4 copy-start.4
  34.2 228.2 %copy-start.7 = (s32[3,512]{1,0:T(4,128)S(1)}, s32[3,512]{1,0:T(4,128)}, u32[]{:S(2)}) copy-start(s32[3,512]{1,0:T(4,128)} %param.17) | copy-start | bytes 18436
  887.2 3.5 copy-start.5
  887.2 3.5 copy-start.11
  892.0 78.5 %copy-start.13 = (f32[256]{0:T(256)S(1)}, f32[256]{0:T(256)}, u32[]{:S(2)}) copy-start(f32[256]{0:T(256)} %param.22) | copy-start | bytes 3076
  970.5 3.1 copy-start.12
Sparse Core Ops, SparseCore 0:
  31.4 849.7 all-reduce.5
  886.4 82.0 all-reduce.7
